TPU v7x, 256 devices: a whole 4x4x8 slice. The times are simulated.
256 devices in a mesh: section: 4 (over z_lo, core), dp: 64 (over y, x, z_hi).
Axes of the slice: x: 4, y: 4, z: 8 (z_hi: 4, z_lo: 2; z = z_hi * 2 + z_lo), core: 2. Of those that a mesh axis runs over, the one named last changes fastest.
Arguments:
- activations_in: bfloat16 [2, 4096, 8192], P(None, 'dp'), may hold values from -6 to 6
- cotangent: bfloat16 [2, 4096, 8192], P(None, 'dp'), may hold values from -6 to 6
- value_tiles: bfloat16 [4, 128, 128, 128], P('section'), may hold values from -0.0625 to 0.0625
- value_ids: int32 [4, 128], P('section'), may hold values from 0 to 255, as said below
- out_tiles: bfloat16 [4, 192, 128, 128], P('section', 'dp'), may hold values from -0.25 to 0.25
- out_ids: int32 [4, 192], P('section'), may hold values from 0 to 255, as said below
- out_count: int32 [4, 64], P('section'), may hold values from 1 to 3, as said below
Outputs:
- section_outputs: bfloat16 [4, 2, 4096, 8192], P('section', None, 'dp')
- input_grads: bfloat16 [4, 2, 4096, 8192], P('section', None, 'dp')
- out_grad: float32 [4, 192, 128, 128], P('section', 'dp')
Inputs may be any that keep to these rules, and one draw needn't show every extreme that they name: `value_ids`: for each layer, 128 different tile numbers. `out_ids`: for each layer, 192 different tile numbers; slot g lies on index g // 3 of dp. The live slots of an index of dp are its first out_count slots; in each layer some index has all 3 slots live.
All inputs are finite; a program needn't handle non-finite values.
Results may differ from a plain program's by a relative error of at most 0.008.
Values may be sent and summed in bfloat16 or wider, within the bound.
No kernel may reach another device: no remote copies, remote signals or barrier semaphores. Data moves between devices by JAX's collectives and lax.ppermute only.
A program may use at most 192 MiB of HBM per device.

v0:
```python
import math

import jax
import jax.numpy as jnp
from jax import lax
from jax.sharding import PartitionSpec as P

VW = 512


def from_behind(value, axis, steps):
    count = lax.axis_size(axis)
    first, last = (max(0, -steps), min(count, count - steps))
    return lax.ppermute(value, axis, [(source, source + steps) for source in range(first, last)])


def build_blocks(tile_data, tile_ids, row_blocks, col_blocks):
    tile_width = tile_data.shape[-1]
    grid = jnp.zeros((row_blocks * col_blocks, tile_width, tile_width), jnp.bfloat16)
    grid = grid.at[tile_ids].set(tile_data)
    return grid.reshape(row_blocks, col_blocks, tile_width, tile_width)


def on_device(activations_in, cotangent, value_tiles, value_ids, out_tiles, out_ids, out_count):
    section_index = lax.axis_index("section")
    section_count = lax.axis_size("section")
    shard_count = lax.axis_size("dp")
    shard_index = lax.axis_index("dp")
    micro_count = activations_in.shape[0]
    tok_rows = activations_in.shape[1]
    model_width = activations_in.shape[2]
    all_rows = micro_count * tok_rows
    tile_width = value_tiles.shape[-1]
    value_width = VW
    value_blocks = value_width // tile_width
    model_blocks = model_width // tile_width
    slot_share = out_tiles.shape[1]
    out_slot = out_ids[0]
    live_mask = (jnp.arange(slot_share, dtype=jnp.int32)[None, :] < out_count[0][:, None]).reshape(
        -1
    )
    own_live = lax.dynamic_slice_in_dim(live_mask, shard_index * slot_share, slot_share)
    gathered = lax.all_gather(out_tiles[0], "dp", axis=0, tiled=True)
    masked_tiles = jnp.where(live_mask[:, None, None], gathered, jnp.zeros_like(gathered))
    value_grid = build_blocks(value_tiles[0], value_ids[0], model_blocks, value_blocks)
    out_grid = build_blocks(masked_tiles, out_slot, value_blocks, model_blocks)

    def forward_layer(operands):
        hidden, old_values, old_result = operands
        hidden_blocked = hidden.reshape(all_rows, model_blocks, tile_width)
        value_rows = jnp.einsum(
            "rbi,bvij->rvj", hidden_blocked, value_grid, preferred_element_type=jnp.float32
        ).astype(jnp.bfloat16)
        update = jnp.einsum(
            "rvi,vmij->rmj", value_rows, out_grid, preferred_element_type=jnp.float32
        ).reshape(all_rows, model_width)
        result = (hidden.astype(jnp.float32) + update).astype(jnp.bfloat16)
        return (value_rows.reshape(all_rows, value_width), result)

    def skip_forward(operands):
        return (operands[1], operands[2])

    def backward_layer(operands):
        grad_rows, old_input = operands
        grad_blocked = grad_rows.reshape(all_rows, model_blocks, tile_width)
        grad_values = jnp.einsum(
            "rmj,vmij->rvi", grad_blocked, out_grid, preferred_element_type=jnp.float32
        ).astype(jnp.bfloat16)
        extra_term = jnp.einsum(
            "rvj,bvij->rbi", grad_values, value_grid, preferred_element_type=jnp.float32
        ).reshape(all_rows, model_width)
        return (grad_rows.astype(jnp.float32) + extra_term).astype(jnp.bfloat16)

    def skip_backward(operands):
        return operands[1]

    first_input = activations_in.reshape(all_rows, model_width)
    value_store = jnp.zeros((all_rows, value_width), jnp.bfloat16)
    act_store = jnp.zeros((all_rows, model_width), jnp.bfloat16)
    carried = jnp.zeros((all_rows, model_width), jnp.bfloat16)
    for step_number in range(section_count):
        active = section_index == step_number
        hidden = jnp.where(section_index == 0, first_input, carried)
        value_store, act_store = lax.cond(
            active, forward_layer, skip_forward, (hidden, value_store, act_store)
        )
        if step_number + 1 < section_count:
            carried = from_behind(act_store, "section", 1)
    last_grad = cotangent.reshape(all_rows, model_width)
    grad_store = jnp.where(section_index == section_count - 1, last_grad, jnp.zeros_like(last_grad))
    input_store = jnp.zeros((all_rows, model_width), jnp.bfloat16)
    carried_grad = jnp.zeros((all_rows, model_width), jnp.bfloat16)
    for step_number in range(section_count):
        active = section_index == section_count - 1 - step_number
        if step_number > 0:
            grad_store = jnp.where(active, carried_grad, grad_store)
        input_store = lax.cond(active, backward_layer, skip_backward, (grad_store, input_store))
        if step_number + 1 < section_count:
            carried_grad = from_behind(input_store, "section", -1)
    grad_scale = 1.0 / math.sqrt(micro_count * tok_rows * shard_count)
    value_blocked = value_store.reshape(all_rows, value_blocks, tile_width)
    grad_blocked = grad_store.reshape(all_rows, model_blocks, tile_width)
    value_part = jnp.take(value_blocked, out_slot // model_blocks, axis=1)
    grad_part = jnp.take(grad_blocked, out_slot % model_blocks, axis=1)
    summed = lax.psum_scatter(
        jnp.einsum("rkc,rkd->kcd", value_part, grad_part, preferred_element_type=jnp.float32),
        "dp",
        scatter_dimension=0,
        tiled=True,
    )
    scaled = summed * grad_scale
    out_grad = jnp.where(own_live[:, None, None], scaled, jnp.zeros_like(scaled))
    section_out = act_store.reshape(micro_count, tok_rows, model_width)
    grad_out = input_store.reshape(micro_count, tok_rows, model_width)
    return (section_out[None], grad_out[None], out_grad[None])


def solution(mesh):
    in_specs = (
        P(None, "dp", None),
        P(None, "dp", None),
        P("section", None, None, None),
        P("section", None),
        P("section", "dp", None, None),
        P("section", None),
        P("section", None),
    )
    out_specs = (
        P("section", None, "dp", None),
        P("section", None, "dp", None),
        P("section", "dp", None, None),
    )
    return jax.shard_map(
        on_device, mesh=mesh, in_specs=in_specs, out_specs=out_specs, check_vma=False
    )
```

profile of v0, /device:TPU:6, one launch (start us, length us, event | category | flops | bytes accessed | tf_op | source)
XLA Modules:
  0.0 639.7 jit_solution(5982883603321064038)
XLA Ops:
  8.0 0.7 iota_compare_fusion
  9.5 5.4 broadcast.209.clone
  14.9 19.4 %scatter_fusion = bf16[256,128,128]{2,1,0:T(8,128)(2,1)} fusion(bf16[256,128,128]{2,1,0:T(8,128)(2,1)} %broadcast.209.clone, s32[128]{0:T(128)S(1)} %fusion.38, bf16[128,128,128]{2,1,0:T(8,128)(2,1)} %bitcast.307), kind=kCustom, calls=%fused_computation.2 | custom fusion | bytes 12583424 | tf_op jit(solution)/shard_map/scatter | solution.py:20
  34.5 78.5 %all-gather.3.cloned.1.call-done = bf16[1,192,128,128]{3,2,0,1:T(8,128)(2,1)} async-done(((bf16[1,3,128,128]{3,2,0,1:T(8,128)(2,1)}), bf16[1,192,128,128]{3,2,0,1:T(8,128)(2,1)}) %all-gather.3.cloned.1.call-update) | async-done | bytes 6291472 | tf_op jit(solution)/shard_map/all_gather | solution.py:43
  113.1 5.9 bitcast_select_fusion
  119.0 5.3 broadcast.209.clone.1
  124.4 28.8 %scatter_fusion.1 = bf16[256,128,128]{2,1,0:T(8,128)(2,1)} fusion(bf16[256,128,128]{2,1,0:T(8,128)(2,1)} %broadcast.209.clone.1, s32[192]{0:T(256)S(1)} %bitcast.312, bf16[192,128,128]{2,1,0:T(8,128)(2,1)} %bitcast_select_fusion), kind=kCustom, calls=%fused_computation.3 | custom fusion | bytes 18875136 | tf_op jit(solution)/shard_map/scatter | solution.py:20
  153.1 1.6 conditional.12
  153.1 1.6 broadcast.201
  154.7 4.2 copy.131
  159.0 1.3 collective-permute-start.3
  160.3 1.6 broadcast_select_fusion.7
  161.8 18.7 %conditional.8 = (bf16[128,512]{0,1:T(8,128)(2,1)}, bf16[128,8192]{0,1:T(8,128)(2,1)}) conditional(s32[]{:T(128)} %convert_element_type.91, () %tuple.76, (bf16[128,8192]{1,0:T(8,128)(2,1)}, bf16[64,4,128,128]{3,2,1,0:T(8,128)(2,1)}, bf16[4,64,128,128]{3,2,1,0:T(8,128)(2,1)}) %tuple.158), branch_computations={%region_2.3_spmd, %region_3.4_spmd} | conditional | flops 2150694912 | bytes 77856840 | solution.py:84
  162.0 4.1 copy.115
  166.1 8.2 %fusion.1 = bf16[128,4,128]{0,2,1:T(8,128)(2,1)} fusion(bf16[128,64,128,1]{0,2,3,1:T(8,128)(2,1)} %bitcast.306, bf16[64,4,128,128]{3,2,1,0:T(8,128)(2,1)} %get-tuple-element.207), kind=kOutput, calls=%fused_computation.7 | convolution fusion | flops 1073807360 | bytes 10616832 | tf_op jit(solution)/shard_map/cond/branch_1_fun/rbi,bvij->rvj/dot_general | solution.py:51
  174.3 4.4 fusion.2
  178.7 1.8 fusion
  180.5 4.1 copy.118
  184.6 2.6 collective-permute-start
  187.2 3.1 broadcast_select_fusion.2
  190.4 4.1 copy.133
  194.4 1.3 collective-permute-start.4
  195.7 1.7 broadcast_select_fusion.6
  197.8 4.1 copy.122
  201.9 25.0 %collective-permute-start.1 = (bf16[128,8192]{1,0:T(8,128)(2,1)}, bf16[128,8192]{1,0:T(8,128)(2,1)}, u32[]{:S(2)}, u32[]{:S(2)}) collective-permute-start(bf16[128,8192]{1,0:T(8,128)(2,1)} %copy.122), channel_id=1, source_target_pairs={{0,64},{64,128},{128,192},{1,65},{65,129},{129,193},{2,66},{66,130... | collective-permute-start | bytes 6291464 | tf_op jit(solution)/shard_map/ppermute | solution.py:14
  226.9 3.1 broadcast_select_fusion.1
  230.0 4.2 conditional.14
  230.0 4.1 copy.191
  234.2 1.3 collective-permute-start.5
  235.6 29.9 %collective-permute-done.5 = bf16[128,8192]{1,0:T(8,128)(2,1)S(1)} collective-permute-done((bf16[128,8192]{1,0:T(8,128)(2,1)}, bf16[128,8192]{1,0:T(8,128)(2,1)S(1)}, u32[]{:S(2)}, u32[]{:S(2)}) %collective-permute-start.5) | collective-permute-done | bytes 2097184 | tf_op jit(solution)/shard_map/ppermute | solution.py:14
  265.5 2.6 broadcast_select_fusion.4
  268.3 27.1 %collective-permute-start.2 = (bf16[128,8192]{0,1:T(8,128)(2,1)}, bf16[128,8192]{0,1:T(8,128)(2,1)}, u32[]{:S(2)}, u32[]{:S(2)}) collective-permute-start(bf16[128,8192]{0,1:T(8,128)(2,1)} %get-tuple-element.131), channel_id=1, source_target_pairs={{0,64},{64,128},{128,192},{1,65},{65,129},{129,193},{2,66},{66,130... | collective-permute-start | bytes 6291464 | tf_op jit(solution)/shard_map/ppermute | solution.py:14
  295.5 4.1 copy.137
  299.5 4.1 copy.138
  303.6 9.6 %gather_fusion.1 = bf16[192,128,128]{2,1,0:T(8,128)(2,1)} fusion(bf16[128,64,128]{2,0,1:T(8,128)(2,1)} %copy.138, s32[1024]{0:T(1024)S(1)} %pad_clamp_fusion), kind=kCustom, calls=%fused_computation.1 | custom fusion | bytes 12583680 | tf_op jit(solution)/shard_map/jit(_take)/gather | solution.py:104
  313.2 1.9 conditional.11
  313.2 1.6 copy.107
  315.1 8.8 %gather_fusion = bf16[192,128,128]{2,1,0:T(8,128)(2,1)} fusion(bf16[128,4,128]{2,0,1:T(8,128)(2,1)} %get-tuple-element.133, s32[1024]{0:T(1024)S(1)} %pad_clamp_fusion.1), kind=kCustom, calls=%fused_computation | custom fusion | bytes 12583680 | tf_op jit(solution)/shard_map/jit(_take)/gather | solution.py:103
  323.9 11.8 %fusion.30 = f32[192,128,128]{2,1,0:T(8,128)} fusion(bf16[192,128,128]{2,1,0:T(8,128)(2,1)} %gather_fusion.1, bf16[192,128,128]{2,1,0:T(8,128)(2,1)} %gather_fusion, pred[192]{0:T(512)(128)(4,1)S(1)} %get-tuple-element.233, pred[192]{0:T(512)(128)(4,1)S(1)} %get-tuple-element.232), kind=kOutput, calls=%fused_computation.51 | convolution fusion | flops 811597824 | bytes 25166208 | tf_op jit(solution)/shard_map/rkc,rkd->kcd/dot_general | solution.py:106
  335.8 1.5 copy-done.9
  337.3 20.6 %conditional.15 = (bf16[1,2,64,8192]{3,2,1,0:T(8,128)(2,1)}) conditional(s32[]{:T(128)} %convert_element_type.91, bf16[128,8192]{1,0:T(8,128)(2,1)} %get-tuple-element.229, (bf16[128,8192]{1,0:T(8,128)(2,1)S(1)}, bf16[4,64,128,128]{3,2,1,0:T(8,128)(2,1)}, bf16[64,4,128,128]{3,2,1,0:T(8,128)(2,1)}) %tuple.167), branch_computations={%region_16.17_spmd, %region_17.18_spmd} | conditional | flops 2150694912 | bytes 73662504 | solution.py:97
  337.6 6.4 fusion.29
  344.0 4.3 fusion.43
  348.3 5.6 copy.113
  353.9 3.9 add_convert_fusion
  357.8 4.1 copy.129
  361.9 268.7 %reduce-scatter.2.cloned.1.call-done = f32[3,128,128]{2,1,0:T(8,128)} async-done(((f32[192,128,128]{2,1,0:T(8,128)}), f32[3,128,128]{2,1,0:T(8,128)}) %reduce-scatter.2.cloned.1.call-update) | async-done | bytes 196624 | tf_op jit(solution)/shard_map/reduce_scatter | solution.py:105
  630.6 1.7 select_bitcast_fusion
  (34 shorter events, 2.5 us)
Async XLA Ops:
  7.2 105.9 %all-gather.3.cloned.1.call-start = ((), (), s32[]{:S(2)}) async-start(), calls=%async_computation.2 | async-start | bytes 6389760 | tf_op jit(solution)/shard_map/all_gather | solution.py:43
  7.9 622.7 %reduce-scatter.2.cloned.1.call-start = ((), (), s32[]{:S(2)}) async-start(), calls=%async_computation.1 | async-start | bytes 12779520 | tf_op jit(solution)/shard_map/reduce_scatter | solution.py:105
  14.9 19.4 %copy-start.16 = (s32[1,192]{1,0:T(1,128)S(1)}, s32[1,192]{1,0:T(1,128)}, u32[]{:S(2)}) copy-start(s32[1,192]{1,0:T(1,128)} %param.28) | copy-start | bytes 2308
  34.5 118.6 %copy-start.8 = (bf16[2,64,8192]{2,1,0:T(8,128)(2,1)}, bf16[2,64,8192]{2,1,0:T(8,128)(2,1)S(1)}, u32[]{:S(2)}) copy-start(bf16[2,64,8192]{2,1,0:T(8,128)(2,1)S(1)} %broadcast_select_fusion.3) | copy-start | bytes 6291460
  154.7 5.5 copy-start.7
  159.0 28.3 %collective-permute-start.3 = (bf16[128,8192]{1,0:T(8,128)(2,1)}, bf16[128,8192]{1,0:T(8,128)(2,1)}, u32[]{:S(2)}, u32[]{:S(2)}) collective-permute-start(bf16[128,8192]{1,0:T(8,128)(2,1)} %copy.131), channel_id=1, source_target_pairs={{64,0},{128,64},{192,128},{65,1},{129,65},{193,129},{66,2},{130,66... | collective-permute-start | bytes 6291464 | tf_op jit(solution)/shard_map/ppermute | solution.py:14
  166.1 8.2 %copy-start.4 = (bf16[4,64,128,128]{3,2,1,0:T(8,128)(2,1)S(1)}, bf16[4,64,128,128]{3,2,1,0:T(8,128)(2,1)}, u32[]{:S(2)}) copy-start(bf16[4,64,128,128]{3,2,1,0:T(8,128)(2,1)} %get-tuple-element.208) | copy-start | bytes 25165828 | tf_op jit(solution)/shard_map/cond
  174.3 4.4 copy-start.15
  184.6 11.2 %collective-permute-start = (bf16[128,8192]{1,0:T(8,128)(2,1)}, bf16[128,8192]{1,0:T(8,128)(2,1)}, u32[]{:S(2)}, u32[]{:S(2)}) collective-permute-start(bf16[128,8192]{1,0:T(8,128)(2,1)} %copy.118), channel_id=1, source_target_pairs={{0,64},{64,128},{128,192},{1,65},{65,129},{129,193},{2,66},{66,130... | collective-permute-start | bytes 6291464 | tf_op jit(solution)/shard_map/ppermute | solution.py:14
  194.4 32.5 %collective-permute-start.4 = (bf16[128,8192]{1,0:T(8,128)(2,1)}, bf16[128,8192]{1,0:T(8,128)(2,1)}, u32[]{:S(2)}, u32[]{:S(2)}) collective-permute-start(bf16[128,8192]{1,0:T(8,128)(2,1)} %copy.133), channel_id=1, source_target_pairs={{64,0},{128,64},{192,128},{65,1},{129,65},{193,129},{66,2},{130,66... | collective-permute-start | bytes 6291464 | tf_op jit(solution)/shard_map/ppermute | solution.py:14
  201.9 33.6 %collective-permute-start.1 = (bf16[128,8192]{1,0:T(8,128)(2,1)}, bf16[128,8192]{1,0:T(8,128)(2,1)}, u32[]{:S(2)}, u32[]{:S(2)}) collective-permute-start(bf16[128,8192]{1,0:T(8,128)(2,1)} %copy.122), channel_id=1, source_target_pairs={{0,64},{64,128},{128,192},{1,65},{65,129},{129,193},{2,66},{66,130... | collective-permute-start | bytes 6291464 | tf_op jit(solution)/shard_map/ppermute | solution.py:14
  234.2 31.2 %collective-permute-start.5 = (bf16[128,8192]{1,0:T(8,128)(2,1)}, bf16[128,8192]{1,0:T(8,128)(2,1)S(1)}, u32[]{:S(2)}, u32[]{:S(2)}) collective-permute-start(bf16[128,8192]{1,0:T(8,128)(2,1)} %get-tuple-element.229), channel_id=1, source_target_pairs={{64,0},{128,64},{192,128},{65,1},{129,65},{193,129},{66,2},{130,66... | collective-permute-start | bytes 6291464 | tf_op jit(solution)/shard_map/ppermute | solution.py:14
  268.3 44.9 %collective-permute-start.2 = (bf16[128,8192]{0,1:T(8,128)(2,1)}, bf16[128,8192]{0,1:T(8,128)(2,1)}, u32[]{:S(2)}, u32[]{:S(2)}) collective-permute-start(bf16[128,8192]{0,1:T(8,128)(2,1)} %get-tuple-element.131), channel_id=1, source_target_pairs={{0,64},{64,128},{128,192},{1,65},{65,129},{129,193},{2,66},{66,130... | collective-permute-start | bytes 6291464 | tf_op jit(solution)/shard_map/ppermute | solution.py:14
  335.7 1.6 copy-start.9
  337.6 6.4 copy-start.3
Sparse Core Ops, SparseCore 0:
  11.2 101.7 all-gather.2
  335.8 294.7 reduce-scatter.1
where the time goes:
time: 649 us; the launch traced here: 640 us
  waiting for transfers between devices  378 us (58%)
  local copies, waits for them, and re-layouts  125 us (19%)
  starting transfers between devices  58.7 us (9%)
  matrix products  35 us (5%)
  other arithmetic  27 us (4%)
  between operations  14.7 us (2%)
    reduce_scatter x1, waiting for transfers between devices, on_device(): lax.psum_scatter(jnp.einsum('rkc,rkd->kcd', value_part, grad_part, prefer...  269 us
    all_gather x1, waiting for transfers between devices, on_device(): gathered = lax.all_gather(out_tiles[0], 'dp', axis=0, tiled=True)  78.5 us
    ppermute x6, starting transfers between devices, from_behind(): lax.ppermute(value, axis, [(source, source + steps) for source in range(f...  58.6 us
    scatter x2, local copies, waits for them, and re-layouts, build_blocks(): grid = grid.at[tile_ids].set(tile_data)  48.2 us
    ppermute x6, waiting for transfers between devices, from_behind(): lax.ppermute(value, axis, [(source, source + steps) for source in range(f...  29.9 us
    another operation x5, local copies, waits for them, and re-layouts  18.1 us
  transfers between devices with their start and end apart: 8, of which 3 were waited for; matrix products, arithmetic and copies ran while one was open for 18% of the time, Pallas kernels for 0%

commit v1 on v0

v1 whole, which is shorter than its diff:
```python
import math

import jax
import jax.numpy as jnp
from jax import lax
from jax.sharding import PartitionSpec as P

VW = 512


def dense_from_tiles(selector, tiles, row_blocks, col_blocks):
    tile_width = tiles.shape[-1]
    grid = jnp.einsum(
        "rck,kij->ricj",
        selector.reshape(row_blocks, col_blocks, -1),
        tiles,
        preferred_element_type=jnp.float32,
    ).astype(jnp.bfloat16)
    return grid.reshape(row_blocks * tile_width, col_blocks * tile_width)


def on_device(activations_in, cotangent, value_tiles, value_ids, out_tiles, out_ids, out_count):
    section_index = lax.axis_index("section")
    section_count = lax.axis_size("section")
    shard_count = lax.axis_size("dp")
    shard_index = lax.axis_index("dp")
    micro_count = activations_in.shape[0]
    tok_rows = activations_in.shape[1]
    model_width = activations_in.shape[2]
    all_rows = micro_count * tok_rows
    tile_width = value_tiles.shape[-1]
    value_width = VW
    value_blocks = value_width // tile_width
    model_blocks = model_width // tile_width
    slot_share = out_tiles.shape[1]
    out_slot = out_ids[0]
    live_mask = (jnp.arange(slot_share, dtype=jnp.int32)[None, :] < out_count[0][:, None]).reshape(
        -1
    )
    own_live = lax.dynamic_slice_in_dim(live_mask, shard_index * slot_share, slot_share)
    gathered = lax.all_gather(out_tiles[0], "dp", axis=0, tiled=True)

    tile_numbers = jnp.arange(value_blocks * model_blocks, dtype=jnp.int32)
    value_select = (value_ids[0][None, :] == tile_numbers[:, None]).astype(jnp.bfloat16)
    value_w = dense_from_tiles(value_select, value_tiles[0], model_blocks, value_blocks)
    out_select = (
        (out_slot[None, :] == tile_numbers[:, None]) & live_mask[None, :]
    ).astype(jnp.bfloat16)
    out_w = dense_from_tiles(out_select, gathered, value_blocks, model_blocks)

    def forward_layer(hidden):
        value_rows = jnp.dot(hidden, value_w, preferred_element_type=jnp.float32).astype(
            jnp.bfloat16
        )
        update = jnp.dot(value_rows, out_w, preferred_element_type=jnp.float32)
        result = (hidden.astype(jnp.float32) + update).astype(jnp.bfloat16)
        return value_rows, result

    def backward_layer(grad_rows):
        grad_values = lax.dot_general(
            grad_rows, out_w, (((1,), (1,)), ((), ())), preferred_element_type=jnp.float32
        ).astype(jnp.bfloat16)
        extra_term = lax.dot_general(
            grad_values, value_w, (((1,), (1,)), ((), ())), preferred_element_type=jnp.float32
        )
        return (grad_rows.astype(jnp.float32) + extra_term).astype(jnp.bfloat16)

    first_input = activations_in.reshape(all_rows, model_width)
    last_grad = cotangent.reshape(all_rows, model_width)
    value_store = jnp.zeros((all_rows, value_width), jnp.bfloat16)
    act_store = jnp.zeros((all_rows, model_width), jnp.bfloat16)
    input_store = jnp.zeros((all_rows, model_width), jnp.bfloat16)
    used_grad = jnp.zeros((all_rows, model_width), jnp.bfloat16)
    forward_in = first_input
    backward_in = last_grad
    for step_number in range(section_count):
        back_section = section_count - 1 - step_number
        value_store, act_store = lax.cond(
            section_index == step_number,
            lambda ops: forward_layer(ops[0]),
            lambda ops: (ops[1], ops[2]),
            (forward_in, value_store, act_store),
        )
        input_store, used_grad = lax.cond(
            section_index == back_section,
            lambda ops: (backward_layer(ops[0]), ops[0]),
            lambda ops: (ops[1], ops[2]),
            (backward_in, input_store, used_grad),
        )
        if step_number + 1 < section_count:
            forward_in = lax.ppermute(act_store, "section", [(step_number, step_number + 1)])
            backward_in = lax.ppermute(
                input_store, "section", [(back_section, back_section - 1)]
            )

    grad_scale = 1.0 / math.sqrt(micro_count * tok_rows * shard_count)
    weight_tiles = jnp.einsum(
        "tri,tcj->rcij",
        value_store.reshape(all_rows, value_blocks, tile_width),
        used_grad.reshape(all_rows, model_blocks, tile_width),
        preferred_element_type=jnp.float32,
    ).astype(jnp.bfloat16)
    weight_tiles = weight_tiles.reshape(value_blocks * model_blocks, tile_width, tile_width)
    picked = jnp.take(weight_tiles, out_slot, axis=0)
    received = lax.all_to_all(
        picked.reshape(shard_count, slot_share, tile_width, tile_width), "dp", 0, 0, tiled=True
    )
    summed = received.astype(jnp.float32).sum(axis=0)
    scaled = summed * grad_scale
    out_grad = jnp.where(own_live[:, None, None], scaled, jnp.zeros_like(scaled))
    section_out = act_store.reshape(micro_count, tok_rows, model_width)
    grad_out = input_store.reshape(micro_count, tok_rows, model_width)
    return (section_out[None], grad_out[None], out_grad[None])


def solution(mesh):
    in_specs = (
        P(None, "dp", None),
        P(None, "dp", None),
        P("section", None, None, None),
        P("section", None),
        P("section", "dp", None, None),
        P("section", None),
        P("section", None),
    )
    out_specs = (
        P("section", None, "dp", None),
        P("section", None, "dp", None),
        P("section", "dp", None, None),
    )
    return jax.shard_map(
        on_device, mesh=mesh, in_specs=in_specs, out_specs=out_specs, check_vma=False
    )
```

time: 649 us -> 454 us (0.70)
  waiting for transfers between devices: 378 us -> 269 us
  local copies, waits for them, and re-layouts: 125 us -> 82.5 us
  starting transfers between devices: 58.7 us -> 21.5 us
  other arithmetic: 27 us -> 11.4 us
  matrix products: 35 us -> 48.3 us
    reduce_scatter x1 -> x0, waiting for transfers between devices: 269 us -> none  [on_device(): lax.psum_scatter(jnp.einsum('rkc,rkd->kcd', value_part, grad_part, prefer...]
    all_to_all x0 -> x1, waiting for transfers between devices: none -> 135 us  [on_device(): lax.all_to_all(picked.reshape(shard_count, slot_share, tile_width, tile_w...]
    scatter x2 -> x0, local copies, waits for them, and re-layouts: 48.2 us -> none  [build_blocks(): grid = grid.at[tile_ids].set(tile_data)]
    ppermute x6, starting transfers between devices: 58.6 us -> 12 us  [the longest x3 6.69 us: on_device(): lax.ppermute(act_store, 'section', [(step_number, step_number + 1)])]
    reshape x2 -> x1, local copies, waits for them, and re-layouts: 9.7 us -> 38.1 us  [dense_from_tiles(): return grid.reshape(row_blocks * tile_width, col_blocks * tile_width)]
    convert_element_type x0 -> x2, local copies, waits for them, and re-layouts: none -> 25.5 us  [the longest x1 13.6 us: dense_from_tiles(): grid = jnp.einsum('rck,kij->ricj', selector.reshape(row_blocks, col_block...]
    cond x12 -> x5, local copies, waits for them, and re-layouts: 24.6 us -> 1.6 us  [the longest x3 12.4 us: on_device(): lax.cond(active, backward_layer, skip_backward, (grad_store, input_store))]
    ppermute x6, waiting for transfers between devices: 29.9 us -> 52.1 us  [the longest x3 51.3 us: on_device(): lax.ppermute(input_store, 'section', [(back_section, back_section - 1)])]
  transfers between devices with their start and end apart: 8 -> 8, of which waited for: 3 -> 4; matrix products, arithmetic and copies ran while one was open for 18% -> 12% of each run, Pallas kernels for 0% -> 0%
where the time goes in v1:
time: 454 us; the launch traced here: 448 us
  waiting for transfers between devices  269 us (59%)
  local copies, waits for them, and re-layouts  82.5 us (18%)
  matrix products  48.3 us (11%)
  starting transfers between devices  21.5 us (5%)
  between operations  14.6 us (3%)
  other arithmetic  11.4 us (3%)
    all_to_all x1, waiting for transfers between devices, on_device(): lax.all_to_all(picked.reshape(shard_count, slot_share, tile_width, tile_w...  135 us
    all_gather x1, waiting for transfers between devices, on_device(): gathered = lax.all_gather(out_tiles[0], 'dp', axis=0, tiled=True)  81.7 us
    ppermute x3, waiting for transfers between devices, on_device(): lax.ppermute(input_store, 'section', [(back_section, back_section - 1)])  51.3 us
    reshape x1, local copies, waits for them, and re-layouts, dense_from_tiles(): return grid.reshape(row_blocks * tile_width, col_blocks * tile_width)  38.1 us
    dot_general x2, matrix products, dense_from_tiles(): jnp.einsum('rck,kij->ricj', selector.reshape(row_blocks, col_blocks, -1),...  17.7 us
    convert_element_type x1, local copies, waits for them, and re-layouts, dense_from_tiles(): grid = jnp.einsum('rck,kij->ricj', selector.reshape(row_blocks, col_block...  13.6 us
    dot_general x1, matrix products, backward_layer(): lax.dot_general(grad_values, value_w, (((1,), (1,)), ((), ())), preferred...  12.4 us
    convert_element_type x1, local copies, waits for them, and re-layouts, on_device(): weight_tiles = jnp.einsum('tri,tcj->rcij', value_store.reshape(all_rows,...  11.9 us
  transfers between devices with their start and end apart: 8, of which 4 were waited for; matrix products, arithmetic and copies ran while one was open for 12% of the time, Pallas kernels for 0%

profile of v1, /device:TPU:6, one launch (start us, length us, event | category | flops | bytes accessed | tf_op | source)
XLA Modules:
  0.0 448.0 jit_solution(13380294247165011361)
XLA Ops:
  7.2 0.0 copy-start.8
  7.2 0.0 all-gather.3.cloned.1.call-start
  7.2 0.7 all-gather.3.cloned.1.call-update
  7.9 0.1 iota_compare_fusion
  8.0 0.2 lt.52
  8.2 9.6 %convert_bitcast_fusion.1 = bf16[64,128,4,128]{3,0,1,2:T(8,128)(2,1)} fusion(bf16[128,128,128]{2,1,0:T(8,128)(2,1)} %bitcast.100, s32[64,4]{0,1:T(4,128)S(1)} %multiply_add_fusion.1, s32[128]{0:T(128)S(1)} %bitcast.104), kind=kOutput, calls=%fused_computation.29 | convolution fusion | flops 1077968896 | bytes 12584448 | tf_op jit(solution)/shard_map/rck,kij->ricj/dot_general | solution.py:13
  17.8 13.6 %copy.29 = bf16[64,128,4,128]{1,0,3,2:T(8,128)(2,1)} copy(bf16[64,128,4,128]{3,0,1,2:T(8,128)(2,1)} %convert_bitcast_fusion.1) | data formatting | bytes 16777216 | tf_op jit(solution)/shard_map/convert_element_type | solution.py:18
  31.4 81.7 %all-gather.3.cloned.1.call-done = bf16[1,192,128,128]{3,2,0,1:T(8,128)(2,1)} async-done(((bf16[1,3,128,128]{3,2,0,1:T(8,128)(2,1)}), bf16[1,192,128,128]{3,2,0,1:T(8,128)(2,1)}) %all-gather.3.cloned.1.call-update) | async-done | bytes 6291472 | tf_op jit(solution)/shard_map/all_gather | solution.py:41
  113.1 8.1 %convolution_convert_fusion.8 = bf16[4,64,128,128]{3,1,2,0:T(8,128)(2,1)S(1)} fusion(bf16[1,192,128,128]{3,2,0,1:T(8,128)(2,1)} %all-gather.3.cloned.1.call-done, s32[4,64]{1,0:T(4,128)S(1)} %multiply_add_fusion, s32[192]{0:T(256)S(1)} %bitcast.102, pred[192]{0:T(512)(128)(4,1)S(1)} %lt.52), kind=kOutput, calls=%fused_computation.30 | convolution fusion | flops 1614905344 | bytes 14682048 | tf_op jit(solution)/shard_map/rck,kij->ricj/dot_general | solution.py:13
  121.2 0.0 copy-start.4
  121.2 38.1 %copy_bitcast_fusion = (bf16[512,8192]{1,0:T(8,128)(2,1)}, bf16[8192,512]{0,1:T(8,128)(2,1)}) fusion(bf16[64,8,64,128]{3,2,1,0:T(8,128)(2,1)S(1)} %bitcast.94, bf16[64,8,64,128]{3,2,1,0:T(8,128)(2,1)} %bitcast.95), kind=kLoop, calls=%fused_computation.26 | loop fusion | bytes 33554432 | tf_op jit(solution)/shard_map/reshape | solution.py:19
  159.3 1.9 conditional.12
  159.3 1.5 broadcast.97
  160.8 0.2 broadcast.97.clone
  161.2 2.0 collective-permute-start.3
  163.2 11.4 %conditional.8 = (bf16[128,512]{1,0:T(8,128)(2,1)}, bf16[128,8192]{1,0:T(8,128)(2,1)}) conditional(s32[]{:T(128)} %convert_element_type.114, () %tuple.88, (bf16[128,8192]{1,0:T(8,128)(2,1)}, bf16[8192,512]{0,1:T(8,128)(2,1)}, bf16[512,8192]{1,0:T(8,128)(2,1)}) %tuple.159), branch_computations={%region_0.0_spmd, %region_1.0_spmd} | conditional | flops 2150694912 | bytes 65273928 | solution.py:78
  163.2 7.7 %convolution_convert_fusion = bf16[128,512]{1,0:T(8,128)(2,1)} fusion(bf16[128,8192]{1,0:T(8,128)(2,1)} %get-tuple-element.96, bf16[8192,512]{0,1:T(8,128)(2,1)} %get-tuple-element.176), kind=kOutput, calls=%fused_computation.3 | convolution fusion | flops 1073807360 | bytes 10616832 | tf_op jit(solution)/shard_map/cond/branch_1_fun/dot_general | solution.py:52
  171.0 3.6 fusion
  174.6 2.6 collective-permute-start
  177.2 0.0 collective-permute-done.3
  177.2 2.0 collective-permute-start.4
  179.2 0.8 collective-permute-done
  180.0 2.0 collective-permute-start.1
  182.0 0.0 collective-permute-done.4
  182.0 0.2 conditional.14
  182.2 1.3 collective-permute-start.5
  183.5 0.0 collective-permute-done.1
  183.5 2.0 collective-permute-start.2
  185.5 0.5 broadcast.105
  186.0 0.6 reduce.3
  186.6 0.1 eq.84
  186.8 51.3 %collective-permute-done.5 = bf16[128,8192]{1,0:T(8,128)(2,1)} collective-permute-done((bf16[128,8192]{1,0:T(8,128)(2,1)}, bf16[128,8192]{1,0:T(8,128)(2,1)}, u32[]{:S(2)}, u32[]{:S(2)}) %collective-permute-start.5) | collective-permute-done | bytes 2097184 | tf_op jit(solution)/shard_map/ppermute | solution.py:92
  238.1 14.0 %conditional.15 = (bf16[1,2,64,8192]{3,2,1,0:T(8,128)(2,1)}, bf16[128,8192]{1,0:T(8,128)(2,1)S(1)}) conditional(s32[]{:T(128)} %convert_element_type.114, (bf16[128,8192]{1,0:T(8,128)(2,1)}, bf16[128,8192]{1,0:T(8,128)(2,1)S(1)}) %get-tuple-element.244, (bf16[128,8192]{1,0:T(8,128)(2,1)}, bf16[512,8192]{1,0:T(8,128)(2,1)}, ...), branch_computations={%region_14.0_spmd, %region_15.0_spmd} | conditional | flops 2150694912 | bytes 25165840 | solution.py:84
  238.1 12.4 %fusion.7 = bf16[128,8192]{1,0:T(8,128)(2,1)} fusion(bf16[8192,512]{0,1:T(8,128)(2,1)} %get-tuple-element.198, bf16[128,8192]{1,0:T(8,128)(2,1)} %get-tuple-element.236, bf16[512,8192]{1,0:T(8,128)(2,1)} %get-tuple-element.118), kind=kOutput, calls=%fused_computation.23 | convolution fusion | flops 2150694912 | bytes 20971520 | tf_op jit(solution)/shard_map/cond/branch_1_fun/dot_general | solution.py:63
  250.5 1.6 copy.107
  252.1 1.9 copy.59
  254.0 0.0 collective-permute-done.2
  254.0 0.2 conditional.11
  254.2 1.3 copy-done.6
  255.6 6.8 %convert_bitcast_fusion = bf16[4,64,128,128]{2,3,0,1:T(8,128)(2,1)} fusion(bf16[128,64,128,1]{2,1,0,3:T(8,128)(2,1)S(1)} %bitcast.99, bf16[128,512]{1,0:T(8,128)(2,1)} %get-tuple-element.200), kind=kOutput, calls=%fused_computation.28 | convolution fusion | flops 1077936128 | bytes 10616832 | tf_op jit(solution)/shard_map/tri,tcj->rcij/dot_general | solution.py:97
  262.4 11.9 %copy.42 = bf16[4,64,128,128]{3,2,1,0:T(8,128)(2,1)} copy(bf16[4,64,128,128]{2,3,0,1:T(8,128)(2,1)} %convert_bitcast_fusion) | data formatting | bytes 16777216 | tf_op jit(solution)/shard_map/convert_element_type | solution.py:102
  274.3 11.5 %gather_fusion = bf16[192,128,128]{2,1,0:T(8,128)(2,1)} fusion(bf16[256,128,128]{2,1,0:T(8,128)(2,1)} %bitcast.96, s32[1024]{0:T(1024)S(1)} %pad_clamp_fusion), kind=kCustom, calls=%fused_computation | custom fusion | bytes 12583680 | tf_op jit(solution)/shard_map/jit(_take)/gather | solution.py:104
  285.8 6.0 %broadcast_select_fusion = bf16[64,3,128,128]{3,2,1,0:T(8,128)(2,1)} fusion(bf16[64,3,128,128]{3,2,1,0:T(8,128)(2,1)} %bitcast.97, pred[64,3]{1,0:T(8,128)(4,1)S(1)} %compare_and_fusion), kind=kLoop, calls=%fused_computation.33 | loop fusion | flops 3145728 | bytes 12583104 | tf_op jit(solution)/shard_map/jit(_take)/select_n | solution.py:104
  291.8 9.5 %all-to-all-start = ((bf16[64,3,128,128]{3,2,1,0:T(8,128)(2,1)}), bf16[64,3,128,128]{3,2,1,0:T(8,128)(2,1)}, u32[]{:S(2)}, u32[]{:S(2)}) async-start(bf16[64,3,128,128]{3,2,1,0:T(8,128)(2,1)} %broadcast_select_fusion), calls=%async_computation | async-start | bytes 12582912 | tf_op jit(solution)/shard_map/all_to_all | solution.py:105
  301.4 0.1 dynamic_slice.3
  301.5 134.6 %all-to-all-done = bf16[64,3,128,128]{3,2,1,0:T(8,128)(2,1)} async-done(((bf16[64,3,128,128]{3,2,1,0:T(8,128)(2,1)}), bf16[64,3,128,128]{3,2,1,0:T(8,128)(2,1)}, u32[]{:S(2)}, u32[]{:S(2)}) %all-to-all-start) | async-done | bytes 6291488 | tf_op jit(solution)/shard_map/all_to_all | solution.py:105
  436.0 3.9 convert_reduce_fusion
  439.9 0.8 bitcast_select_fusion
  (19 shorter events, 0.1 us)
Async XLA Ops:
  7.2 1.0 copy-start.8
  7.2 0.8 copy-start.9
  7.2 105.9 %all-gather.3.cloned.1.call-start = ((), (), s32[]{:S(2)}) async-start(), calls=%async_computation.1 | async-start | bytes 6389760 | tf_op jit(solution)/shard_map/all_gather | solution.py:41
  17.8 95.3 %copy-start.7 = (s32[1,192]{1,0:T(1,128)S(1)}, s32[1,192]{1,0:T(1,128)}, u32[]{:S(2)}) copy-start(s32[1,192]{1,0:T(1,128)} %param.28) | copy-start | bytes 2308
  121.2 38.1 %copy-start.4 = (bf16[2,64,8192]{2,1,0:T(8,128)(2,1)S(1)}, bf16[2,64,8192]{2,1,0:T(8,128)(2,1)}, u32[]{:S(2)}) copy-start(bf16[2,64,8192]{2,1,0:T(8,128)(2,1)} %param.24) | copy-start | bytes 6291460
  161.2 16.0 %collective-permute-start.3 = (bf16[128,8192]{1,0:T(8,128)(2,1)}, bf16[128,8192]{1,0:T(8,128)(2,1)}, u32[]{:S(2)}, u32[]{:S(2)}) collective-permute-start(bf16[128,8192]{1,0:T(8,128)(2,1)} %get-tuple-element.137), channel_id=1, source_target_pairs={{192,128},{193,129},{194,130},{195,131},{196,132},{197,133},{198,1... | collective-permute-start | bytes 6291464 | tf_op jit(solution)/shard_map/ppermute | solution.py:92
  163.2 7.7 %copy-start = (bf16[512,8192]{1,0:T(8,128)(2,1)S(1)}, bf16[512,8192]{1,0:T(8,128)(2,1)}, u32[]{:S(2)}) copy-start(bf16[512,8192]{1,0:T(8,128)(2,1)} %get-tuple-element.98) | copy-start | bytes 25165828 | tf_op jit(solution)/shard_map/cond
  163.2 7.7 %copy-start.5 = (bf16[128,8192]{1,0:T(8,128)(2,1)S(1)}, bf16[128,8192]{1,0:T(8,128)(2,1)}, u32[]{:S(2)}) copy-start(bf16[128,8192]{1,0:T(8,128)(2,1)} %get-tuple-element.96) | copy-start | bytes 6291460 | tf_op jit(solution)/shard_map/cond
  174.6 5.4 %collective-permute-start = (bf16[128,8192]{1,0:T(8,128)(2,1)}, bf16[128,8192]{1,0:T(8,128)(2,1)}, u32[]{:S(2)}, u32[]{:S(2)}) collective-permute-start(bf16[128,8192]{1,0:T(8,128)(2,1)} %get-tuple-element.133), channel_id=1, source_target_pairs={{0,64},{1,65},{2,66},{3,67},{4,68},{5,69},{6,70},{7,71},{8,72},{9,... | collective-permute-start | bytes 6291464 | tf_op jit(solution)/shard_map/ppermute | solution.py:91
  177.2 4.8 %collective-permute-start.4 = (bf16[128,8192]{1,0:T(8,128)(2,1)}, bf16[128,8192]{1,0:T(8,128)(2,1)}, u32[]{:S(2)}, u32[]{:S(2)}) collective-permute-start(bf16[128,8192]{1,0:T(8,128)(2,1)} %get-tuple-element.138), channel_id=1, source_target_pairs={{128,64},{129,65},{130,66},{131,67},{132,68},{133,69},{134,70},{13... | collective-permute-start | bytes 6291464 | tf_op jit(solution)/shard_map/ppermute | solution.py:92
  180.0 3.5 collective-permute-start.1
  182.2 55.9 %collective-permute-start.5 = (bf16[128,8192]{1,0:T(8,128)(2,1)}, bf16[128,8192]{1,0:T(8,128)(2,1)}, u32[]{:S(2)}, u32[]{:S(2)}) collective-permute-start(bf16[128,8192]{1,0:T(8,128)(2,1)} %get-tuple-element.239), channel_id=1, source_target_pairs={{64,0},{65,1},{66,2},{67,3},{68,4},{69,5},{70,6},{71,7},{72,8},{73... | collective-permute-start | bytes 6291464 | tf_op jit(solution)/shard_map/ppermute | solution.py:92
  183.5 70.5 %collective-permute-start.2 = (bf16[128,8192]{1,0:T(8,128)(2,1)}, bf16[128,8192]{1,0:T(8,128)(2,1)}, u32[]{:S(2)}, u32[]{:S(2)}) collective-permute-start(bf16[128,8192]{1,0:T(8,128)(2,1)} %get-tuple-element.238), channel_id=1, source_target_pairs={{128,192},{129,193},{130,194},{131,195},{132,196},{133,197},{134,1... | collective-permute-start | bytes 6291464 | tf_op jit(solution)/shard_map/ppermute | solution.py:91
  254.0 1.6 copy-start.6
  291.8 144.2 %all-to-all-start = ((bf16[64,3,128,128]{3,2,1,0:T(8,128)(2,1)}), bf16[64,3,128,128]{3,2,1,0:T(8,128)(2,1)}, u32[]{:S(2)}, u32[]{:S(2)}) async-start(bf16[64,3,128,128]{3,2,1,0:T(8,128)(2,1)} %broadcast_select_fusion), calls=%async_computation | async-start | bytes 12582912 | tf_op jit(solution)/shard_map/all_to_all | solution.py:105
Sparse Core Ops, SparseCore 0:
  11.3 101.7 all-gather.2

commit v2 on v1

--- a/solution.py
+++ b/solution.py
@@ -3,20 +3,78 @@
 import jax
 import jax.numpy as jnp
 from jax import lax
+from jax.experimental import pallas as pl
+from jax.experimental.pallas import tpu as pltpu
 from jax.sharding import PartitionSpec as P
 
 VW = 512
+INTERPRET = False
 
 
-def dense_from_tiles(selector, tiles, row_blocks, col_blocks):
+def place_tiles(source, tiles, row_blocks, col_blocks, rows_per_step):
     tile_width = tiles.shape[-1]
-    grid = jnp.einsum(
-        "rck,kij->ricj",
-        selector.reshape(row_blocks, col_blocks, -1),
-        tiles,
-        preferred_element_type=jnp.float32,
-    ).astype(jnp.bfloat16)
-    return grid.reshape(row_blocks * tile_width, col_blocks * tile_width)
+
+    def kernel(source_ref, tiles_ref, out_ref):
+        step = pl.program_id(0)
+        for row in range(rows_per_step):
+            for col in range(col_blocks):
+                pick = source_ref[(step * rows_per_step + row) * col_blocks + col]
+                tile = tiles_ref[jnp.maximum(pick, 0)]
+                tile = jnp.where(pick >= 0, tile, jnp.zeros_like(tile))
+                out_ref[
+                    row * tile_width : (row + 1) * tile_width,
+                    col * tile_width : (col + 1) * tile_width,
+                ] = tile
+
+    grid_spec = pltpu.PrefetchScalarGridSpec(
+        num_scalar_prefetch=1,
+        grid=(row_blocks // rows_per_step,),
+        in_specs=[pl.BlockSpec(tiles.shape, lambda step, src: (0, 0, 0))],
+        out_specs=pl.BlockSpec(
+            (rows_per_step * tile_width, col_blocks * tile_width), lambda step, src: (step, 0)
+        ),
+    )
+    return pl.pallas_call(
+        kernel,
+        grid_spec=grid_spec,
+        out_shape=jax.ShapeDtypeStruct(
+            (row_blocks * tile_width, col_blocks * tile_width), tiles.dtype
+        ),
+        interpret=INTERPRET,
+    )(source, tiles)
+
+
+def tile_products(tile_ids, left_t, right, col_blocks, slots_per_step):
+    slot_count = tile_ids.shape[0]
+    tile_width = right.shape[-1]
+
+    def kernel(ids_ref, left_ref, right_ref, out_ref):
+        step = pl.program_id(0)
+        for slot in range(slots_per_step):
+            tile = ids_ref[step * slots_per_step + slot]
+            out_ref[slot] = jnp.dot(
+                left_ref[tile // col_blocks],
+                right_ref[tile % col_blocks],
+                preferred_element_type=jnp.float32,
+            )
+
+    grid_spec = pltpu.PrefetchScalarGridSpec(
+        num_scalar_prefetch=1,
+        grid=(slot_count // slots_per_step,),
+        in_specs=[
+            pl.BlockSpec(left_t.shape, lambda step, ids: (0, 0, 0)),
+            pl.BlockSpec(right.shape, lambda step, ids: (0, 0, 0)),
+        ],
+        out_specs=pl.BlockSpec(
+            (slots_per_step, tile_width, tile_width), lambda step, ids: (step, 0, 0)
+        ),
+    )
+    return pl.pallas_call(
+        kernel,
+        grid_spec=grid_spec,
+        out_shape=jax.ShapeDtypeStruct((slot_count, tile_width, tile_width), jnp.float32),
+        interpret=INTERPRET,
+    )(tile_ids, left_t, right)
 
 
 def on_device(activations_in, cotangent, value_tiles, value_ids, out_tiles, out_ids, out_count):
@@ -41,12 +99,21 @@
     gathered = lax.all_gather(out_tiles[0], "dp", axis=0, tiled=True)
 
     tile_numbers = jnp.arange(value_blocks * model_blocks, dtype=jnp.int32)
-    value_select = (value_ids[0][None, :] == tile_numbers[:, None]).astype(jnp.bfloat16)
-    value_w = dense_from_tiles(value_select, value_tiles[0], model_blocks, value_blocks)
-    out_select = (
-        (out_slot[None, :] == tile_numbers[:, None]) & live_mask[None, :]
-    ).astype(jnp.bfloat16)
-    out_w = dense_from_tiles(out_select, gathered, value_blocks, model_blocks)
+    value_order = jnp.arange(value_ids.shape[1], dtype=jnp.int32)
+    value_source = jnp.max(
+        jnp.where(value_ids[0][None, :] == tile_numbers[:, None], value_order[None, :], -1), axis=1
+    )
+    value_w = place_tiles(value_source, value_tiles[0], model_blocks, value_blocks, 8)
+    slot_order = jnp.arange(out_slot.shape[0], dtype=jnp.int32)
+    out_source = jnp.max(
+        jnp.where(
+            (out_slot[None, :] == tile_numbers[:, None]) & live_mask[None, :],
+            slot_order[None, :],
+            -1,
+        ),
+        axis=1,
+    )
+    out_w = place_tiles(out_source, gathered, value_blocks, model_blocks, 1)
 
     def forward_layer(hidden):
         value_rows = jnp.dot(hidden, value_w, preferred_element_type=jnp.float32).astype(
@@ -94,14 +161,9 @@
             )
 
     grad_scale = 1.0 / math.sqrt(micro_count * tok_rows * shard_count)
-    weight_tiles = jnp.einsum(
-        "tri,tcj->rcij",
-        value_store.reshape(all_rows, value_blocks, tile_width),
-        used_grad.reshape(all_rows, model_blocks, tile_width),
-        preferred_element_type=jnp.float32,
-    ).astype(jnp.bfloat16)
-    weight_tiles = weight_tiles.reshape(value_blocks * model_blocks, tile_width, tile_width)
-    picked = jnp.take(weight_tiles, out_slot, axis=0)
+    values_t = value_store.reshape(all_rows, value_blocks, tile_width).transpose(1, 2, 0)
+    grad_cols = used_grad.reshape(all_rows, model_blocks, tile_width).transpose(1, 0, 2)
+    picked = tile_products(out_slot, values_t, grad_cols, model_blocks, 16).astype(jnp.bfloat16)
     received = lax.all_to_all(
         picked.reshape(shard_count, slot_share, tile_width, tile_width), "dp", 0, 0, tiled=True
     )

time: 454 us -> 395 us (0.87)
  local copies, waits for them, and re-layouts: 82.5 us -> 12.7 us
  Pallas kernels: 0 us -> 27.4 us
  matrix products: 48.3 us -> 23.5 us
  waiting for transfers between devices: 269 us -> 279 us
    reshape x1, local copies, waits for them, and re-layouts: 38.1 us -> 4.05 us  [on_device(): used_grad.reshape(all_rows, model_blocks, tile_width).transpose(1, 0, 2)]
    pallas_call x0 -> x3, Pallas kernels: none -> 27.4 us  [the longest x2 16.8 us: place_tiles(): pl.pallas_call(kernel, grid_spec=grid_spec, out_shape=jax.ShapeDtypeStruc...]
    convert_element_type x2 -> x0, local copies, waits for them, and re-layouts: 25.5 us -> none  [the longest x1 13.6 us: dense_from_tiles(): grid = jnp.einsum('rck,kij->ricj', selector.reshape(row_blocks, col_block...]
    dot_general x3 -> x0, matrix products: 24.5 us -> none  [the longest x2 17.7 us: dense_from_tiles(): jnp.einsum('rck,kij->ricj', selector.reshape(row_blocks, col_blocks, -1),...]
    all_gather x1, waiting for transfers between devices: 81.7 us -> 95 us  [on_device(): gathered = lax.all_gather(out_tiles[0], 'dp', axis=0, tiled=True)]
    gather x1 -> x0, local copies, waits for them, and re-layouts: 11.5 us -> none  [on_device(): picked = jnp.take(weight_tiles, out_slot, axis=0)]
    all_to_all x1, waiting for transfers between devices: 135 us -> 124 us  [on_device(): lax.all_to_all(picked.reshape(shard_count, slot_share, tile_width, tile_w...]
    convert_element_type x0 -> x1, other arithmetic: none -> 8.77 us  [on_device(): tile_products(out_slot, values_t, grad_cols, model_blocks, 16)]
  transfers between devices with their start and end apart: 8 -> 8, of which waited for: 4 -> 4; matrix products, arithmetic and copies ran while one was open for 12% -> 8% of each run, Pallas kernels for 0% -> 2%
where the time goes in v2:
time: 395 us; the launch traced here: 393 us
  waiting for transfers between devices  279 us (71%)
  Pallas kernels  27.4 us (7%)
  matrix products  23.5 us (6%)
  starting transfers between devices  21.4 us (5%)
  other arithmetic  14.9 us (4%)
  between operations  14.1 us (4%)
  local copies, waits for them, and re-layouts  12.7 us (3%)
    all_to_all x1, waiting for transfers between devices, on_device(): lax.all_to_all(picked.reshape(shard_count, slot_share, tile_width, tile_w...  124 us
    all_gather x1, waiting for transfers between devices, on_device(): gathered = lax.all_gather(out_tiles[0], 'dp', axis=0, tiled=True)  95 us
    ppermute x3, waiting for transfers between devices, on_device(): lax.ppermute(input_store, 'section', [(back_section, back_section - 1)])  58 us
    pallas_call x2, Pallas kernels, place_tiles(): pl.pallas_call(kernel, grid_spec=grid_spec, out_shape=jax.ShapeDtypeStruc...  16.8 us
    dot_general x1, matrix products, backward_layer(): lax.dot_general(grad_values, value_w, (((1,), (1,)), ((), ())), preferred...  13.9 us
    pallas_call x1, Pallas kernels, tile_products(): pl.pallas_call(kernel, grid_spec=grid_spec, out_shape=jax.ShapeDtypeStruc...  10.6 us
    all_to_all x1, starting transfers between devices, on_device(): lax.all_to_all(picked.reshape(shard_count, slot_share, tile_width, tile_w...  9.54 us
    convert_element_type x1, other arithmetic, on_device(): tile_products(out_slot, values_t, grad_cols, model_blocks, 16)  8.77 us
  transfers between devices with their start and end apart: 8, of which 4 were waited for; matrix products, arithmetic and copies ran while one was open for 8% of the time, Pallas kernels for 2%

profile of v2, /device:TPU:6, one launch (start us, length us, event | category | flops | bytes accessed | tf_op | source)
XLA Modules:
  0.0 392.6 jit_solution(13910188274743323661)
XLA Ops:
  7.2 0.0 copy-start.8
  7.2 0.0 copy-start.7
  7.2 0.0 all-gather.3.cloned.1.call-start
  7.2 0.7 all-gather.3.cloned.1.call-update
  7.9 0.0 copy-done.7
  7.9 0.1 iota_compare_fusion.2
  8.0 0.2 lt.30
  8.2 0.0 copy-done.8
  8.2 0.7 select_reduce_fusion.1.source_ref
  8.9 8.5 %shard_map.94 = bf16[8192,512]{1,0:T(8,128)(2,1)} custom-call(s32[256]{0:T(256)} %select_reduce_fusion.1.source_ref, bf16[128,128,128]{2,1,0:T(8,128)(2,1)} %bitcast.54), custom_call_target="tpu_custom_call" | custom-call | tf_op jit(solution)/shard_map/pallas_call | solution.py:37
  17.4 0.0 copy-done.6
  17.4 0.7 select_reduce_fusion.source_ref
  18.1 95.0 %all-gather.3.cloned.1.call-done = bf16[1,192,128,128]{3,2,0,1:T(8,128)(2,1)} async-done(((bf16[1,3,128,128]{3,2,0,1:T(8,128)(2,1)}), bf16[1,192,128,128]{3,2,0,1:T(8,128)(2,1)}) %all-gather.3.cloned.1.call-update) | async-done | bytes 6291472 | tf_op jit(solution)/shard_map/all_gather | solution.py:99
  113.1 8.3 %shard_map.95 = bf16[512,8192]{1,0:T(8,128)(2,1)} custom-call(s32[256]{0:T(256)} %select_reduce_fusion.source_ref, bf16[192,128,128]{2,1,0:T(8,128)(2,1)} %bitcast.53), custom_call_target="tpu_custom_call" | custom-call | tf_op jit(solution)/shard_map/pallas_call | solution.py:37
  121.3 0.0 copy-done.4
  121.3 1.7 conditional.12
  121.3 0.2 broadcast.35.clone
  121.5 1.5 broadcast.35
  123.1 2.0 collective-permute-start.3
  125.0 10.5 %conditional.8 = (bf16[128,512]{1,0:T(8,128)(2,1)}, bf16[128,8192]{1,0:T(8,128)(2,1)}) conditional(s32[]{:T(128)} %convert_element_type.97, () %tuple.76, (bf16[128,8192]{1,0:T(8,128)(2,1)}, bf16[8192,512]{1,0:T(8,128)(2,1)}, bf16[512,8192]{1,0:T(8,128)(2,1)}) %tuple.121), branch_computations={%region_2.3_spmd, %region_3.4_spmd} | conditional | flops 2150694912 | bytes 65273928 | solution.py:145
  125.0 6.1 %convolution_convert_fusion = bf16[128,512]{1,0:T(8,128)(2,1)} fusion(bf16[128,8192]{1,0:T(8,128)(2,1)} %get-tuple-element.87, bf16[8192,512]{1,0:T(8,128)(2,1)} %get-tuple-element.88), kind=kOutput, calls=%fused_computation.2 | convolution fusion | flops 1073807360 | bytes 10616832 | tf_op jit(solution)/shard_map/cond/branch_1_fun/dot_general | solution.py:119
  131.1 0.3 copy-done
  131.4 0.6 copy-done.5
  132.1 3.5 fusion
  135.5 2.6 collective-permute-start
  138.2 0.0 collective-permute-done.3
  138.2 2.0 collective-permute-start.4
  140.2 0.8 collective-permute-done
  140.9 2.0 collective-permute-start.1
  142.9 0.0 collective-permute-done.4
  143.0 1.3 collective-permute-start.5
  144.2 0.0 collective-permute-done.1
  144.3 2.0 collective-permute-start.2
  146.3 58.0 %collective-permute-done.5 = bf16[128,8192]{1,0:T(8,128)(2,1)} collective-permute-done((bf16[128,8192]{1,0:T(8,128)(2,1)}, bf16[128,8192]{1,0:T(8,128)(2,1)}, u32[]{:S(2)}, u32[]{:S(2)}) %collective-permute-start.5) | collective-permute-done | bytes 2097184 | tf_op jit(solution)/shard_map/ppermute | solution.py:159
  204.3 15.5 %conditional.15 = (bf16[128,8192]{1,0:T(8,128)(2,1)S(1)}, bf16[1,2,64,8192]{3,2,1,0:T(8,128)(2,1)}) conditional(s32[]{:T(128)} %convert_element_type.97, (bf16[128,8192]{1,0:T(8,128)(2,1)S(1)}, bf16[128,8192]{1,0:T(8,128)(2,1)}) %tuple.109, (bf16[128,8192]{1,0:T(8,128)(2,1)}, bf16[512,8192]{1,0:T(8,128)(2,1)}, bf16[8192,512]{1,0:T(8,128)(2,1)}) %tuple.86), branch_computations={%region_16.17_spmd, %region_17.18_spmd} | conditional | flops 2150694912 | bytes 25165840 | solution.py:151
  204.3 13.9 %fusion.7 = bf16[128,8192]{1,0:T(8,128)(2,1)} fusion(bf16[8192,512]{1,0:T(8,128)(2,1)} %get-tuple-element.110, bf16[128,8192]{1,0:T(8,128)(2,1)} %get-tuple-element.172, bf16[512,8192]{1,0:T(8,128)(2,1)} %get-tuple-element.109), kind=kOutput, calls=%fused_computation.22 | convolution fusion | flops 2150694912 | bytes 20971520 | tf_op jit(solution)/shard_map/cond/branch_1_fun/dot_general | solution.py:130
  218.2 1.6 copy.52
  219.8 2.4 copy.20
  222.2 4.1 %copy.21 = bf16[128,64,128]{2,0,1:T(8,128)(2,1)} copy(bf16[128,64,128]{0,2,1:T(8,128)(2,1)} %bitcast.51) | data formatting | bytes 4194304 | tf_op jit(solution)/shard_map/reshape | solution.py:165
  226.3 0.0 collective-permute-done.2
  226.3 1.7 copy.19
  228.0 10.6 %shard_map.96 = f32[192,128,128]{2,1,0:T(8,128)} custom-call(s32[192]{0:T(256)} %bitcast.57, bf16[4,128,128]{2,1,0:T(8,128)(2,1)} %bitcast.55, bf16[64,128,128]{2,1,0:T(8,128)(2,1)} %bitcast.52), custom_call_target="tpu_custom_call" | custom-call | tf_op jit(solution)/shard_map/pallas_call | solution.py:72
  238.6 8.8 %convert_element_type.98 = bf16[192,128,128]{2,1,0:T(8,128)(2,1)} convert(f32[192,128,128]{2,1,0:T(8,128)} %shard_map.96) | non-fusion elementwise | flops 3145728 | bytes 18874368 | tf_op jit(solution)/shard_map/convert_element_type | solution.py:166
  247.3 9.5 %all-to-all-start = ((bf16[64,3,128,128]{3,2,1,0:T(8,128)(2,1)}), bf16[64,3,128,128]{3,2,1,0:T(8,128)(2,1)}, u32[]{:S(2)}, u32[]{:S(2)}) async-start(bf16[64,3,128,128]{3,2,1,0:T(8,128)(2,1)} %bitcast.48), calls=%async_computation | async-start | bytes 12582912 | tf_op jit(solution)/shard_map/all_to_all | solution.py:167
  256.9 0.1 dynamic_slice.3
  257.0 124.1 %all-to-all-done = bf16[64,3,128,128]{3,2,1,0:T(8,128)(2,1)} async-done(((bf16[64,3,128,128]{3,2,1,0:T(8,128)(2,1)}), bf16[64,3,128,128]{3,2,1,0:T(8,128)(2,1)}, u32[]{:S(2)}, u32[]{:S(2)}) %all-to-all-start) | async-done | bytes 6291488 | tf_op jit(solution)/shard_map/all_to_all | solution.py:167
  381.1 3.9 convert_reduce_fusion
  385.0 0.8 bitcast_select_fusion
  (9 shorter events, 0.0 us)
Async XLA Ops:
  7.2 1.0 copy-start.8
  7.2 0.8 copy-start.7
  7.2 105.9 %all-gather.3.cloned.1.call-start = ((), (), s32[]{:S(2)}) async-start(), calls=%async_computation.1 | async-start | bytes 6389760 | tf_op jit(solution)/shard_map/all_gather | solution.py:99
  8.9 8.5 %copy-start.6 = (s32[1,192]{1,0:T(1,128)S(1)}, s32[1,192]{1,0:T(1,128)}, u32[]{:S(2)}) copy-start(s32[1,192]{1,0:T(1,128)} %param.28) | copy-start | bytes 2308
  113.1 8.3 %copy-start.4 = (bf16[2,64,8192]{2,1,0:T(8,128)(2,1)S(1)}, bf16[2,64,8192]{2,1,0:T(8,128)(2,1)}, u32[]{:S(2)}) copy-start(bf16[2,64,8192]{2,1,0:T(8,128)(2,1)} %param.24) | copy-start | bytes 6291460
  123.1 15.1 %collective-permute-start.3 = (bf16[128,8192]{1,0:T(8,128)(2,1)}, bf16[128,8192]{1,0:T(8,128)(2,1)}, u32[]{:S(2)}, u32[]{:S(2)}) collective-permute-start(bf16[128,8192]{1,0:T(8,128)(2,1)} %get-tuple-element.129), channel_id=1, source_target_pairs={{192,128},{193,129},{194,130},{195,131},{196,132},{197,133},{198,1... | collective-permute-start | bytes 6291464 | tf_op jit(solution)/shard_map/ppermute | solution.py:159
  125.0 6.4 %copy-start = (bf16[512,8192]{1,0:T(8,128)(2,1)S(1)}, bf16[512,8192]{1,0:T(8,128)(2,1)}, u32[]{:S(2)}) copy-start(bf16[512,8192]{1,0:T(8,128)(2,1)} %get-tuple-element.89) | copy-start | bytes 25165828 | tf_op jit(solution)/shard_map/cond
  125.0 7.0 %copy-start.5 = (bf16[128,8192]{1,0:T(8,128)(2,1)S(1)}, bf16[128,8192]{1,0:T(8,128)(2,1)}, u32[]{:S(2)}) copy-start(bf16[128,8192]{1,0:T(8,128)(2,1)} %get-tuple-element.87) | copy-start | bytes 6291460 | tf_op jit(solution)/shard_map/cond
  135.5 5.4 %collective-permute-start = (bf16[128,8192]{1,0:T(8,128)(2,1)}, bf16[128,8192]{1,0:T(8,128)(2,1)}, u32[]{:S(2)}, u32[]{:S(2)}) collective-permute-start(bf16[128,8192]{1,0:T(8,128)(2,1)} %get-tuple-element.125), channel_id=1, source_target_pairs={{0,64},{1,65},{2,66},{3,67},{4,68},{5,69},{6,70},{7,71},{8,72},{9,... | collective-permute-start | bytes 6291464 | tf_op jit(solution)/shard_map/ppermute | solution.py:158
  138.2 4.8 %collective-permute-start.4 = (bf16[128,8192]{1,0:T(8,128)(2,1)}, bf16[128,8192]{1,0:T(8,128)(2,1)}, u32[]{:S(2)}, u32[]{:S(2)}) collective-permute-start(bf16[128,8192]{1,0:T(8,128)(2,1)} %get-tuple-element.130), channel_id=1, source_target_pairs={{128,64},{129,65},{130,66},{131,67},{132,68},{133,69},{134,70},{13... | collective-permute-start | bytes 6291464 | tf_op jit(solution)/shard_map/ppermute | solution.py:159
  140.9 3.3 collective-permute-start.1
  143.0 61.3 %collective-permute-start.5 = (bf16[128,8192]{1,0:T(8,128)(2,1)}, bf16[128,8192]{1,0:T(8,128)(2,1)}, u32[]{:S(2)}, u32[]{:S(2)}) collective-permute-start(bf16[128,8192]{1,0:T(8,128)(2,1)} %get-tuple-element.177), channel_id=1, source_target_pairs={{64,0},{65,1},{66,2},{67,3},{68,4},{69,5},{70,6},{71,7},{72,8},{73... | collective-permute-start | bytes 6291464 | tf_op jit(solution)/shard_map/ppermute | solution.py:159
  144.3 82.0 %collective-permute-start.2 = (bf16[128,8192]{1,0:T(8,128)(2,1)}, bf16[128,8192]{1,0:T(8,128)(2,1)}, u32[]{:S(2)}, u32[]{:S(2)}) collective-permute-start(bf16[128,8192]{1,0:T(8,128)(2,1)} %get-tuple-element.175), channel_id=1, source_target_pairs={{128,192},{129,193},{130,194},{131,195},{132,196},{133,197},{134,1... | collective-permute-start | bytes 6291464 | tf_op jit(solution)/shard_map/ppermute | solution.py:158
  247.3 133.8 %all-to-all-start = ((bf16[64,3,128,128]{3,2,1,0:T(8,128)(2,1)}), bf16[64,3,128,128]{3,2,1,0:T(8,128)(2,1)}, u32[]{:S(2)}, u32[]{:S(2)}) async-start(bf16[64,3,128,128]{3,2,1,0:T(8,128)(2,1)} %bitcast.48), calls=%async_computation | async-start | bytes 12582912 | tf_op jit(solution)/shard_map/all_to_all | solution.py:167
Sparse Core Ops, SparseCore 0:
  11.3 101.7 all-gather.2
